TPU v7x, 256 devices: a whole 4x4x8 slice. The times are simulated.
256 devices in a mesh: row: 64 (over z, y, core), col: 4 (over x).
Axes of the slice: x: 4, y: 4, z: 8, core: 2. Of those that a mesh axis runs over, the one named last changes fastest.
Arguments:
- panel_adj: float32 [24576, 512], P('row', 'col'), may hold values from -16 to 16
- inv_tile: float32 [512, 512], P('col'), may hold values from -1 to 2, as said below
- factor_panel: float32 [24576, 512], P('row', 'col'), may hold values from -0.0390625 to 0.0390625
- block_row: float32 [512, 8192], P('row', 'col'), may hold values from -0.25 to 0.25
- slab: float32 [24576, 8192], P('row', 'col'), may hold values from -0.0390625 to 0.0390625
- slab_adj: float32 [24576, 8192], P('row', 'col'), may hold values from -6 to 6
- row_adj: float32 [512, 8192], P('row', 'col'), may hold values from -6 to 6
- diag_adj: float32 [512, 512], P('row', 'col'), may hold values from -6 to 6
Outputs:
- panel_out: float32 [24576, 512], P('row', 'col')
- slab_out: float32 [24576, 8192], P('row', 'col')
- row_out: float32 [512, 8192], P('row', 'col')
- diag_out: float32 [512, 512], P('row', 'col')
Inputs may be any that keep to these rules, and one draw needn't show every extreme that they name: inv_tile is lower triangular with diagonal entries between 1 and 2.
All inputs are finite; a program needn't handle non-finite values.
Results may differ from a plain program's by a relative error of at most 0.00011.
Values sent between devices are 32-bit elements; how exact they have to be, the bound alone decides.
No kernel may reach another device: no remote copies, remote signals or barrier semaphores. Data moves between devices by JAX's collectives and lax.ppermute only.
A program may use at most 64 MiB of HBM per device.

v0:
```python
import jax
import jax.numpy as jnp
from jax import lax
from jax.sharding import PartitionSpec as P


def contract_rows(left, right):
    return lax.dot_general(
        left,
        right,
        (((0,), (0,)), ((), ())),
        precision=lax.Precision.HIGHEST,
        preferred_element_type=jnp.float32,
    )


def per_device(panel_adj, inv_tile, factor_panel, block_row, slab, slab_adj, row_adj, diag_adj):
    precise = lax.Precision.HIGHEST
    col_width = panel_adj.shape[1]
    col_place = lax.axis_index("col")
    share = diag_adj.shape[0]
    partial_panel = jnp.dot(
        panel_adj, inv_tile, precision=precise, preferred_element_type=jnp.float32
    )
    scaled = lax.psum(partial_panel, "col")
    panel_out = lax.dynamic_slice_in_dim(scaled, col_place * col_width, col_width, 1)
    slab_out = slab_adj - jnp.dot(
        scaled,
        lax.all_gather(block_row, "row", axis=0, tiled=True),
        precision=precise,
        preferred_element_type=jnp.float32,
    )
    row_term = lax.psum_scatter(contract_rows(scaled, slab), "row", scatter_dimension=0, tiled=True)
    diag_term = lax.psum_scatter(
        contract_rows(scaled, factor_panel), "row", scatter_dimension=0, tiled=True
    )
    row_ids = lax.broadcasted_iota(jnp.int32, diag_adj.shape, 0) + lax.axis_index("row") * share
    col_ids = lax.broadcasted_iota(jnp.int32, diag_adj.shape, 1) + col_place * col_width
    diag_out = diag_adj - jnp.where(col_ids <= row_ids, diag_term, 0.0)
    return (panel_out, slab_out, row_adj - row_term, diag_out)


def solution(mesh):
    return jax.shard_map(
        per_device,
        mesh=mesh,
        in_specs=(
            P("row", "col"),
            P("col", None),
            P("row", "col"),
            P("row", "col"),
            P("row", "col"),
            P("row", "col"),
            P("row", "col"),
            P("row", "col"),
        ),
        out_specs=(P("row", "col"), P("row", "col"), P("row", "col"), P("row", "col")),
        check_vma=False,
    )
```

profile of v0, /device:TPU:1, one launch (start us, length us, event | category | flops | bytes accessed | tf_op | source)
XLA Modules:
  0.0 371.2 jit_solution(2602399601953829121)
XLA Ops:
  7.2 0.0 copy-start
  7.2 0.0 all-reduce.6.cloned.1.call-start
  7.2 2.8 fusion.1
  10.1 0.0 all-reduce.6.cloned.1.call-update
  10.1 0.0 copy-start.2
  10.1 0.0 all-reduce.8.cloned.1.call-start
  10.2 52.2 %all-reduce.6.cloned.1.call-done = f32[384,512]{1,0:T(8,128)} async-done(((f32[384,512]{1,0:T(8,128)}), f32[384,512]{1,0:T(8,128)}) %all-reduce.6.cloned.1.call-update) | async-done | bytes 786448 | tf_op jit(solution)/shard_map/psum | solution.py:25
  62.4 0.0 copy-done
  62.4 0.0 copy-start.1
  62.4 9.5 %fusion.2 = f32[512,2048]{1,0:T(8,128)} fusion(f32[384,512]{1,0:T(8,128)} %all-reduce.6.cloned.1.call-done, f32[384,2048]{1,0:T(8,128)S(1)} %copy-done), kind=kOutput, calls=%fused_computation.8 | convolution fusion | flops 4831838208 | bytes 8126464 | tf_op jit(solution)/shard_map/dot_general | solution.py:8
  71.8 0.0 copy-done.2
  71.8 0.0 copy-done.1
  71.8 0.0 copy-start.5
  71.9 0.0 copy-start.4
  71.9 0.0 copy-start.3
  71.9 2.2 fusion.3
  74.1 0.0 all-reduce.8.cloned.1.call-update
  74.1 0.0 all-gather.2.cloned.1.call-start
  74.2 0.7 all-gather.2.cloned.1.call-update
  74.9 0.0 copy-done.5
  74.9 0.6 dynamic-slice
  76.1 1.6 constant_dynamic-slice_fusion
  77.8 194.3 %all-reduce.8.cloned.1.call-done = (f32[512,2048]{1,0:T(8,128)}, f32[512,128]{1,0:T(8,128)}) async-done(((f32[512,2048]{1,0:T(8,128)}, f32[512,128]{1,0:T(8,128)}), (f32[512,2048]{1,0:T(8,128)}, f32[512,128]{1,0:T(8,128)})) %all-reduce.8.cloned.1.call-update) | async-done | bytes 4456464
  272.1 0.0 copy-done.4
  272.1 1.3 fusion
  273.4 0.0 copy-done.3
  273.4 1.5 dynamic-slice_subtract_fusion
  274.9 80.2 %all-gather.2.cloned.1.call-done = f32[512,2048]{1,0:T(8,128)} async-done(((f32[8,2048]{1,0:T(8,128)}), f32[512,2048]{1,0:T(8,128)}) %all-gather.2.cloned.1.call-update) | async-done | bytes 4194320 | tf_op jit(solution)/shard_map/all_gather | solution.py:29
  355.1 9.6 %convolution_subtract_fusion = f32[384,2048]{1,0:T(8,128)} fusion(f32[384,2048]{1,0:T(8,128)} %param.13, f32[384,512]{1,0:T(8,128)} %all-reduce.6.cloned.1.call-done, f32[512,2048]{1,0:T(8,128)} %all-gather.2.cloned.1.call-done), kind=kOutput, calls=%fused_computation | convolution fusion | flops 4832624640 | bytes 11272192 | tf_op jit(solution)/shard_map/dot_general | solution.py:27
  (2 shorter events, 0.0 us)
Async XLA Ops:
  7.2 55.2 %copy-start = (f32[384,2048]{1,0:T(8,128)S(1)}, f32[384,2048]{1,0:T(8,128)}, u32[]{:S(2)}) copy-start(f32[384,2048]{1,0:T(8,128)} %param.12) | copy-start | bytes 9437188
  7.2 55.2 %all-reduce.6.cloned.1.call-start = ((), (), s32[]{:S(2)}) async-start(), calls=%async_computation | async-start | bytes 1572864 | tf_op jit(solution)/shard_map/psum | solution.py:25
  10.1 61.7 %copy-start.2 = (f32[384,128]{1,0:T(8,128)S(1)}, f32[384,128]{1,0:T(8,128)}, u32[]{:S(2)}) copy-start(f32[384,128]{1,0:T(8,128)} %param.10) | copy-start | bytes 589828
  10.1 262.0 %all-reduce.8.cloned.1.call-start = ((), (), s32[]{:S(2)}) async-start(), calls=%async_computation.2 | async-start | bytes 8912896
  62.4 9.5 %copy-start.1 = (f32[384,512]{1,0:T(8,128)S(1)}, f32[384,512]{1,0:T(8,128)}, u32[]{:S(2)}) copy-start(f32[384,512]{1,0:T(8,128)} %all-reduce.6.cloned.1.call-done) | copy-start | bytes 2359300
  71.8 3.0 copy-start.5
  71.9 200.2 %copy-start.4 = (f32[8,128]{1,0:T(8,128)S(1)}, f32[8,128]{1,0:T(8,128)}, u32[]{:S(2)}) copy-start(f32[8,128]{1,0:T(8,128)} %param.15) | copy-start | bytes 12292
  71.9 201.6 %copy-start.3 = (f32[8,2048]{1,0:T(8,128)S(1)}, f32[8,2048]{1,0:T(8,128)}, u32[]{:S(2)}) copy-start(f32[8,2048]{1,0:T(8,128)} %param.14) | copy-start | bytes 196612
  74.1 280.9 %all-gather.2.cloned.1.call-start = ((), (), s32[]{:S(2)}) async-start(), calls=%async_computation.1 | async-start | bytes 4259840 | tf_op jit(solution)/shard_map/all_gather | solution.py:29
Sparse Core Ops, SparseCore 0:
  10.9 51.3 all-reduce.5
  74.2 197.7 all-reduce.7
  274.9 80.1 all-gather.1
where the time goes:
time: 371 us
  waiting for transfers between devices  327 us (88%)
  matrix products  24.1 us (6%)
  between operations  14.5 us (4%)
    unnamed x4, waiting for transfers between devices  195 us
    all_gather x1, waiting for transfers between devices, per_device(): lax.all_gather(block_row, 'row', axis=0, tiled=True)  80.2 us
    psum x1, waiting for transfers between devices, per_device(): scaled = lax.psum(partial_panel, 'col')  52.2 us
    dot_general x2, matrix products, contract_rows(): lax.dot_general(left, right, (((0,), (0,)), ((), ())), precision=lax.Prec...  11.7 us
    dot_general x1, matrix products, per_device(): jnp.dot(scaled, lax.all_gather(block_row, 'row', axis=0, tiled=True), pre...  9.61 us
  transfers between devices with their start and end apart: 3, of which 3 were waited for; matrix products, arithmetic and copies ran while one was open for 1% of the time, Pallas kernels for 0%

commit v1 on v0

--- a/solution.py
+++ b/solution.py
@@ -2,6 +2,13 @@
 import jax.numpy as jnp
 from jax import lax
 from jax.sharding import PartitionSpec as P
+
+
+def show_leaf_here(local, k_dim=0):
+    leaves = []
+    for _ in range(lax.psum(1, "row")):
+        leaves.append(local)
+    return jnp.concatenate(lax.all_to_all(jnp.stack(leaves, axis=0), "row", 0, 0), axis=k_dim)
 
 
 def contract_rows(left, right):
@@ -25,10 +32,7 @@
     scaled = lax.psum(partial_panel, "col")
     panel_out = lax.dynamic_slice_in_dim(scaled, col_place * col_width, col_width, 1)
     slab_out = slab_adj - jnp.dot(
-        scaled,
-        lax.all_gather(block_row, "row", axis=0, tiled=True),
-        precision=precise,
-        preferred_element_type=jnp.float32,
+        scaled, show_leaf_here(block_row), precision=precise, preferred_element_type=jnp.float32
     )
     row_term = lax.psum_scatter(contract_rows(scaled, slab), "row", scatter_dimension=0, tiled=True)
     diag_term = lax.psum_scatter(

time: 371 us -> 313 us (0.84)
  waiting for transfers between devices: 327 us -> 250 us
  starting transfers between devices: 0.12 us -> 13.5 us
  local copies, waits for them, and re-layouts: 2.25 us -> 6.34 us
    all_gather x1 -> x0, waiting for transfers between devices: 80.2 us -> none  [per_device(): lax.all_gather(block_row, 'row', axis=0, tiled=True)]
    all_to_all x0 -> x1, starting transfers between devices: none -> 13.5 us  [show_leaf_here(): lax.all_to_all(jnp.stack(leaves, axis=0), 'row', 0, 0)]
    unnamed x4 -> x3, waiting for transfers between devices: 195 us -> 199 us
  transfers between devices with their start and end apart: 3 -> 3, of which waited for: 3 -> 2; matrix products, arithmetic and copies ran while one was open for 1% -> 7% of each run, Pallas kernels for 0% -> 0%
where the time goes in v1:
time: 313 us; the launch traced here: 312 us
  waiting for transfers between devices  250 us (80%)
  matrix products  24.9 us (8%)
  between operations  14.7 us (5%)
  starting transfers between devices  13.5 us (4%)
  local copies, waits for them, and re-layouts  6.34 us (2%)
    unnamed x3, waiting for transfers between devices  199 us
    psum x1, waiting for transfers between devices, per_device(): scaled = lax.psum(partial_panel, 'col')  50.4 us
    all_to_all x1, starting transfers between devices, show_leaf_here(): lax.all_to_all(jnp.stack(leaves, axis=0), 'row', 0, 0)  13.5 us
    dot_general x2, matrix products, contract_rows(): lax.dot_general(left, right, (((0,), (0,)), ((), ())), precision=lax.Prec...  12.7 us
    dot_general x1, matrix products, per_device(): jnp.dot(scaled, show_leaf_here(block_row), precision=precise, preferred_e...  9.61 us
  transfers between devices with their start and end apart: 3, of which 2 were waited for; matrix products, arithmetic and copies ran while one was open for 7% of the time, Pallas kernels for 0%

profile of v1, /device:TPU:1, one launch (start us, length us, event | category | flops | bytes accessed | tf_op | source)
XLA Modules:
  0.0 312.1 jit_solution(11668526658773828954)
XLA Ops:
  7.2 0.0 copy-start
  7.2 3.5 %stack.2 = f32[64,8,2048]{2,1,0:T(8,128)} broadcast(f32[8,2048]{1,0:T(8,128)} %param.11), dimensions={1,2} | broadcast | bytes 4259840 | tf_op jit(solution)/shard_map/stack | solution.py:11
  10.7 0.0 copy-start.1
  10.7 13.5 %all-to-all-start = ((f32[64,8,2048]{2,1,0:T(8,128)}), f32[64,8,2048]{2,1,0:T(8,128)}, u32[]{:S(2)}, u32[]{:S(2)}) async-start(f32[64,8,2048]{2,1,0:T(8,128)} %stack.2), calls=%async_computation | async-start | bytes 8388608 | tf_op jit(solution)/shard_map/all_to_all | solution.py:11
  24.1 0.0 all-reduce.6.cloned.1.call-start
  24.2 0.0 copy-done.1
  24.2 2.6 fusion.6
  26.8 0.0 all-reduce.6.cloned.1.call-update
  26.8 0.0 all-reduce.8.cloned.1.call-start
  26.8 50.4 %all-reduce.6.cloned.1.call-done = f32[384,512]{1,0:T(8,128)} async-done(((f32[384,512]{1,0:T(8,128)}), f32[384,512]{1,0:T(8,128)}) %all-reduce.6.cloned.1.call-update) | async-done | bytes 786448 | tf_op jit(solution)/shard_map/psum | solution.py:32
  77.3 3.3 %fusion.8 = f32[512,128]{1,0:T(8,128)} fusion(f32[384,512]{1,0:T(8,128)} %all-reduce.6.cloned.1.call-done, f32[384,128]{1,0:T(8,128)} %param.10), kind=kOutput, calls=%fused_computation.11 | convolution fusion | flops 301989888 | bytes 1245184 | tf_op jit(solution)/shard_map/dot_general | solution.py:15
  80.6 0.0 copy-done
  80.6 9.4 %fusion.7 = f32[512,2048]{1,0:T(8,128)} fusion(f32[384,512]{1,0:T(8,128)} %all-reduce.6.cloned.1.call-done, f32[384,2048]{1,0:T(8,128)S(1)} %copy-done), kind=kOutput, calls=%fused_computation.10 | convolution fusion | flops 4831838208 | bytes 8126464 | tf_op jit(solution)/shard_map/dot_general | solution.py:15
  90.0 0.0 copy-start.4
  90.0 0.0 copy-start.3
  90.0 0.0 copy-start.2
  90.0 0.0 all-reduce.8.cloned.1.call-update
  90.0 0.6 copy-done.4
  90.7 0.6 dynamic-slice
  91.9 1.6 constant_dynamic-slice_fusion
  93.5 199.3 %all-reduce.8.cloned.1.call-done = (f32[512,2048]{1,0:T(8,128)}, f32[512,128]{1,0:T(8,128)}) async-done(((f32[512,2048]{1,0:T(8,128)}, f32[512,128]{1,0:T(8,128)}), (f32[512,2048]{1,0:T(8,128)}, f32[512,128]{1,0:T(8,128)})) %all-reduce.8.cloned.1.call-update) | async-done | bytes 4456464
  292.8 0.0 copy-done.3
  292.8 1.3 fusion.5
  294.1 0.0 copy-done.2
  294.1 1.5 dynamic-slice_subtract_fusion
  295.6 0.0 all-to-all-done
  295.6 9.6 %fusion.2 = f32[384,2048]{1,0:T(8,128)} fusion(f32[384,2048]{1,0:T(8,128)} %param.13, f32[384,512]{1,0:T(8,128)} %all-reduce.6.cloned.1.call-done, f32[64,8,2048]{2,1,0:T(8,128)} %all-to-all-done), kind=kOutput, calls=%fused_computation.2 | convolution fusion | flops 4832624640 | bytes 11272192 | tf_op jit(solution)/shard_map/dot_general | solution.py:34
  (2 shorter events, 0.0 us)
Async XLA Ops:
  7.2 73.4 %copy-start = (f32[384,2048]{1,0:T(8,128)S(1)}, f32[384,2048]{1,0:T(8,128)}, u32[]{:S(2)}) copy-start(f32[384,2048]{1,0:T(8,128)} %param.12) | copy-start | bytes 9437188
  10.7 13.5 %copy-start.1 = (f32[128,512]{1,0:T(8,128)S(1)}, f32[128,512]{1,0:T(8,128)}, u32[]{:S(2)}) copy-start(f32[128,512]{1,0:T(8,128)} %param.9) | copy-start | bytes 786436
  10.7 285.0 %all-to-all-start = ((f32[64,8,2048]{2,1,0:T(8,128)}), f32[64,8,2048]{2,1,0:T(8,128)}, u32[]{:S(2)}, u32[]{:S(2)}) async-start(f32[64,8,2048]{2,1,0:T(8,128)} %stack.2), calls=%async_computation | async-start | bytes 8388608 | tf_op jit(solution)/shard_map/all_to_all | solution.py:11
  24.1 53.1 %all-reduce.6.cloned.1.call-start = ((), (), s32[]{:S(2)}) async-start(), calls=%async_computation.1 | async-start | bytes 1572864 | tf_op jit(solution)/shard_map/psum | solution.py:32
  26.8 266.0 %all-reduce.8.cloned.1.call-start = ((), (), s32[]{:S(2)}) async-start(), calls=%async_computation.2 | async-start | bytes 8912896
  90.0 0.7 copy-start.4
  90.0 202.8 %copy-start.3 = (f32[8,128]{1,0:T(8,128)S(1)}, f32[8,128]{1,0:T(8,128)}, u32[]{:S(2)}) copy-start(f32[8,128]{1,0:T(8,128)} %param.15) | copy-start | bytes 12292
  90.0 204.2 %copy-start.2 = (f32[8,2048]{1,0:T(8,128)S(1)}, f32[8,2048]{1,0:T(8,128)}, u32[]{:S(2)}) copy-start(f32[8,2048]{1,0:T(8,128)} %param.14) | copy-start | bytes 196612
Sparse Core Ops, SparseCore 0:
  27.9 49.3 all-reduce.5
  90.1 202.6 all-reduce.7

commit v2 on v0

--- a/solution.py
+++ b/solution.py
@@ -2,6 +2,17 @@
 import jax.numpy as jnp
 from jax import lax
 from jax.sharding import PartitionSpec as P
+
+
+def put_stages_all(t0):
+    parts_n = lax.axis_size("col")
+    y1 = lambda block_last: [(dev, dev ^ block_last) for dev in range(parts_n)]
+    near = t0
+    for d in range(parts_n.bit_length() - 1):
+        v_next = y1(1 << d)
+        before = lax.ppermute(near, "col", perm=v_next)
+        near = near + before
+    return near
 
 
 def contract_rows(left, right):
@@ -22,7 +33,7 @@
     partial_panel = jnp.dot(
         panel_adj, inv_tile, precision=precise, preferred_element_type=jnp.float32
     )
-    scaled = lax.psum(partial_panel, "col")
+    scaled = put_stages_all(partial_panel)
     panel_out = lax.dynamic_slice_in_dim(scaled, col_place * col_width, col_width, 1)
     slab_out = slab_adj - jnp.dot(
         scaled,

time: 371 us -> 358 us (0.965)
  waiting for transfers between devices: 327 us -> 309 us
  starting transfers between devices: 0.12 us -> 6.23 us
    psum x1 -> x0, waiting for transfers between devices: 52.2 us -> none  [per_device(): scaled = lax.psum(partial_panel, 'col')]
    ppermute x0 -> x2, waiting for transfers between devices: none -> 32.1 us  [put_stages_all(): before = lax.ppermute(near, 'col', perm=v_next)]
    ppermute x0 -> x2, starting transfers between devices: none -> 6.15 us  [put_stages_all(): before = lax.ppermute(near, 'col', perm=v_next)]
    unnamed x4 -> x3, waiting for transfers between devices: 195 us -> 197 us
  transfers between devices with their start and end apart: 3 -> 4, of which waited for: 3 -> 4; matrix products, arithmetic and copies ran while one was open for 1% -> 1% of each run, Pallas kernels for 0% -> 0%
where the time goes in v2:
time: 358 us
  waiting for transfers between devices  309 us (86%)
  matrix products  22.1 us (6%)
  between operations  14.8 us (4%)
  starting transfers between devices  6.23 us (2%)
    unnamed x3, waiting for transfers between devices  197 us
    all_gather x1, waiting for transfers between devices, per_device(): lax.all_gather(block_row, 'row', axis=0, tiled=True)  80.1 us
    ppermute x2, waiting for transfers between devices, put_stages_all(): before = lax.ppermute(near, 'col', perm=v_next)  32.1 us
    dot_general x2, matrix products, contract_rows(): lax.dot_general(left, right, (((0,), (0,)), ((), ())), precision=lax.Prec...  10.6 us
    dot_general x1, matrix products, per_device(): jnp.dot(scaled, lax.all_gather(block_row, 'row', axis=0, tiled=True), pre...  9.61 us
  transfers between devices with their start and end apart: 4, of which 4 were waited for; matrix products, arithmetic and copies ran while one was open for 1% of the time, Pallas kernels for 0%

profile of v2, /device:TPU:1, one launch (start us, length us, event | category | flops | bytes accessed | tf_op | source)
XLA Modules:
  0.0 357.8 jit_solution(14183771679890586457)
XLA Ops:
  7.2 0.0 copy-start
  7.2 0.0 all-reduce.5.cloned.1.call-start
  7.2 2.0 fusion.1
  9.2 2.1 collective-permute-start
  11.3 16.0 %collective-permute-done = f32[384,512]{1,0:T(8,128)S(1)} collective-permute-done((f32[384,512]{1,0:T(8,128)S(1)}, f32[384,512]{1,0:T(8,128)S(1)}, u32[]{:S(2)}, u32[]{:S(2)}) %collective-permute-start) | collective-permute-done | bytes 786464 | tf_op jit(solution)/shard_map/ppermute | solution.py:13
  27.3 0.1 add.27
  27.5 4.0 %collective-permute-start.1 = (f32[384,512]{1,0:T(8,128)S(1)}, f32[384,512]{1,0:T(8,128)S(1)}, u32[]{:S(2)}, u32[]{:S(2)}) collective-permute-start(f32[384,512]{1,0:T(8,128)S(1)} %add.27), channel_id=1, source_target_pairs={{0,2},{1,3},{2,0},{3,1},{4,6},{5,7},{6,4},{7,5},{8,10},{9,11},{10,... | collective-permute-start | bytes 2359304 | tf_op jit(solution)/shard_map/ppermute | solution.py:13
  31.5 16.1 %collective-permute-done.1 = f32[384,512]{1,0:T(8,128)S(1)} collective-permute-done((f32[384,512]{1,0:T(8,128)S(1)}, f32[384,512]{1,0:T(8,128)S(1)}, u32[]{:S(2)}, u32[]{:S(2)}) %collective-permute-start.1) | collective-permute-done | bytes 786464 | tf_op jit(solution)/shard_map/ppermute | solution.py:13
  47.6 0.1 add.28
  47.8 0.0 copy-done
  47.8 0.0 copy-start.1
  47.8 0.0 copy-start.2
  47.8 8.4 %fusion.2 = f32[512,2048]{1,0:T(8,128)} fusion(f32[384,512]{1,0:T(8,128)S(1)} %add.28, f32[384,2048]{1,0:T(8,128)S(1)} %copy-done), kind=kOutput, calls=%fused_computation.8 | convolution fusion | flops 4831838208 | bytes 8126464 | tf_op jit(solution)/shard_map/dot_general | solution.py:19
  56.2 0.0 copy-done.1
  56.2 0.0 copy-done.2
  56.2 0.0 copy-start.5
  56.2 0.0 copy-start.4
  56.2 0.0 copy-start.3
  56.2 2.2 fusion.3
  58.4 0.0 all-reduce.5.cloned.1.call-update
  58.4 0.0 all-gather.2.cloned.1.call-start
  58.5 0.7 all-gather.2.cloned.1.call-update
  59.2 0.0 copy-done.5
  59.2 0.6 dynamic-slice
  60.4 1.6 constant_dynamic-slice_fusion
  62.1 196.3 %all-reduce.5.cloned.1.call-done = (f32[512,2048]{1,0:T(8,128)}, f32[512,128]{1,0:T(8,128)}) async-done(((f32[512,2048]{1,0:T(8,128)}, f32[512,128]{1,0:T(8,128)}), (f32[512,2048]{1,0:T(8,128)}, f32[512,128]{1,0:T(8,128)})) %all-reduce.5.cloned.1.call-update) | async-done | bytes 4456464
  258.4 0.0 copy-done.4
  258.4 1.3 fusion
  259.8 0.0 copy-done.3
  259.8 1.5 dynamic-slice_subtract_fusion
  261.2 80.1 %all-gather.2.cloned.1.call-done = f32[512,2048]{1,0:T(8,128)} async-done(((f32[8,2048]{1,0:T(8,128)}), f32[512,2048]{1,0:T(8,128)}) %all-gather.2.cloned.1.call-update) | async-done | bytes 4194320 | tf_op jit(solution)/shard_map/all_gather | solution.py:40
  341.4 9.6 %convolution_subtract_fusion = f32[384,2048]{1,0:T(8,128)} fusion(f32[384,2048]{1,0:T(8,128)} %param.13, f32[384,512]{1,0:T(8,128)} %copy-done.1, f32[512,2048]{1,0:T(8,128)} %all-gather.2.cloned.1.call-done), kind=kOutput, calls=%fused_computation | convolution fusion | flops 4832624640 | bytes 11272192 | tf_op jit(solution)/shard_map/dot_general | solution.py:38
  (2 shorter events, 0.0 us)
Async XLA Ops:
  7.2 40.6 %copy-start = (f32[384,2048]{1,0:T(8,128)S(1)}, f32[384,2048]{1,0:T(8,128)}, u32[]{:S(2)}) copy-start(f32[384,2048]{1,0:T(8,128)} %param.12) | copy-start | bytes 9437188
  7.2 251.2 %all-reduce.5.cloned.1.call-start = ((), (), s32[]{:S(2)}) async-start(), calls=%async_computation.1 | async-start | bytes 8912896
  9.2 18.1 %collective-permute-start = (f32[384,512]{1,0:T(8,128)S(1)}, f32[384,512]{1,0:T(8,128)S(1)}, u32[]{:S(2)}, u32[]{:S(2)}) collective-permute-start(f32[384,512]{1,0:T(8,128)S(1)} %fusion.1), channel_id=1, source_target_pairs={{0,1},{1,0},{2,3},{3,2},{4,5},{5,4},{6,7},{7,6},{8,9},{9,8},{10,11... | collective-permute-start | bytes 2359304 | tf_op jit(solution)/shard_map/ppermute | solution.py:13
  27.5 20.2 %collective-permute-start.1 = (f32[384,512]{1,0:T(8,128)S(1)}, f32[384,512]{1,0:T(8,128)S(1)}, u32[]{:S(2)}, u32[]{:S(2)}) collective-permute-start(f32[384,512]{1,0:T(8,128)S(1)} %add.27), channel_id=1, source_target_pairs={{0,2},{1,3},{2,0},{3,1},{4,6},{5,7},{6,4},{7,5},{8,10},{9,11},{10,... | collective-permute-start | bytes 2359304 | tf_op jit(solution)/shard_map/ppermute | solution.py:13
  47.8 8.4 %copy-start.1 = (f32[384,512]{1,0:T(8,128)}, f32[384,512]{1,0:T(8,128)S(1)}, u32[]{:S(2)}) copy-start(f32[384,512]{1,0:T(8,128)S(1)} %add.28) | copy-start | bytes 2359300
  47.8 8.4 %copy-start.2 = (f32[384,128]{1,0:T(8,128)S(1)}, f32[384,128]{1,0:T(8,128)}, u32[]{:S(2)}) copy-start(f32[384,128]{1,0:T(8,128)} %param.10) | copy-start | bytes 589828
  56.2 3.0 copy-start.5
  56.2 202.2 %copy-start.4 = (f32[8,128]{1,0:T(8,128)S(1)}, f32[8,128]{1,0:T(8,128)}, u32[]{:S(2)}) copy-start(f32[8,128]{1,0:T(8,128)} %param.15) | copy-start | bytes 12292
  56.2 203.6 %copy-start.3 = (f32[8,2048]{1,0:T(8,128)S(1)}, f32[8,2048]{1,0:T(8,128)}, u32[]{:S(2)}) copy-start(f32[8,2048]{1,0:T(8,128)} %param.14) | copy-start | bytes 196612
  58.4 283.0 %all-gather.2.cloned.1.call-start = ((), (), s32[]{:S(2)}) async-start(), calls=%async_computation | async-start | bytes 4259840 | tf_op jit(solution)/shard_map/all_gather | solution.py:40
Sparse Core Ops, SparseCore 0:
  58.5 199.8 all-reduce.4
  261.2 80.1 all-gather.1
